TPU v7x, 128 devices: a whole 4x4x4 slice. The times are simulated.
128 devices in a mesh: rep: 4 (over z), shard: 32 (over x, y, core).
Axes of the slice: x: 4, y: 4, z: 4, core: 2. Of those that a mesh axis runs over, the one named last changes fastest.
Arguments:
- trained_sq: float32 [4, 4, 768, 768], P('rep', None, 'shard'), may hold values from -6 to 6
- trained_up: float32 [4, 768, 3072], P('rep', 'shard'), may hold values from -6 to 6
- trained_down: float32 [4, 3072, 768], P('rep', 'shard'), may hold values from -6 to 6
- trained_ln: float32 [4, 4, 768], P('rep', None, 'shard'), may hold values from -6 to 6
- start_sq: float32 [4, 768, 768], P(None, 'shard'), may hold values from -6 to 6
- start_up: float32 [768, 3072], P('shard'), may hold values from -6 to 6
- start_down: float32 [3072, 768], P('shard'), may hold values from -6 to 6
- start_ln: float32 [4, 768], P(None, 'shard'), may hold values from -6 to 6
- resid_sq: float32 [4, 4, 768, 768], P('rep', None, 'shard'), may hold values from -4 to 4
- resid_up: float32 [4, 768, 3072], P('rep', 'shard'), may hold values from -4 to 4
- resid_down: float32 [4, 3072, 768], P('rep', 'shard'), may hold values from -4 to 4
- mom_sq: float32 [4, 768, 768], P(None, 'shard'), may hold values from -3 to 3
- mom_up: float32 [768, 3072], P('shard'), may hold values from -3 to 3
- mom_down: float32 [3072, 768], P('shard'), may hold values from -3 to 3
- mom_ln: float32 [4, 768], P(None, 'shard'), may hold values from -3 to 3
- basis_sq: float32 [4, 768, 64], replicated, may hold values from -0.21875 to 0.21875
- basis_up: float32 [3072, 64], replicated, may hold values from -0.109375 to 0.109375
- basis_down: float32 [768, 64], replicated, may hold values from -0.21875 to 0.21875
Outputs:
- new_resid_sq: float32 [4, 4, 768, 768], P('rep', None, 'shard')
- new_resid_up: float32 [4, 768, 3072], P('rep', 'shard')
- new_resid_down: float32 [4, 3072, 768], P('rep', 'shard')
- new_mom_sq: float32 [4, 768, 768], P(None, 'shard')
- new_mom_up: float32 [768, 3072], P('shard')
- new_mom_down: float32 [3072, 768], P('shard')
- new_mom_ln: float32 [4, 768], P(None, 'shard')
- weights_sq: bfloat16 [4, 768, 768], replicated
- weights_up: bfloat16 [768, 3072], replicated
- weights_down: bfloat16 [3072, 768], replicated
- weights_ln: bfloat16 [4, 768], replicated
All inputs are finite; a program needn't handle non-finite values.
Results may differ from a plain program's by a relative error of at most 0.001.
Values may be sent and summed in bfloat16 or wider, within the bound.
No kernel may reach another device: no remote copies, remote signals or barrier semaphores. Data moves between devices by JAX's collectives and lax.ppermute only.
A program may use at most 128 MiB of HBM per device.

v0:
```python
import jax
import jax.numpy as jnp
from jax import lax
from jax.sharding import PartitionSpec as P

moment_coef = 0.9
outer_rate = 0.7


def advance(start, moment, outer):
    new_moment = moment_coef * moment + outer
    weights = (start - outer_rate * (outer + moment_coef * new_moment)).astype(jnp.bfloat16)
    return (new_moment, weights)


def on_device(
    trained_sq,
    trained_up,
    trained_down,
    trained_ln,
    start_sq,
    start_up,
    start_down,
    start_ln,
    resid_sq,
    resid_up,
    resid_down,
    mom_sq,
    mom_up,
    mom_down,
    mom_ln,
    basis_sq,
    basis_up,
    basis_down,
):
    highest = lax.Precision.HIGHEST
    groups = lax.axis_size("rep")
    delta_sq = start_sq - trained_sq[0] + resid_sq[0]
    factor_sq = jnp.einsum("mrd,mdk->mrk", delta_sq, basis_sq, precision=highest)
    new_resid_sq = delta_sq - jnp.einsum("mrk,mdk->mrd", factor_sq, basis_sq, precision=highest)
    delta_up = start_up - trained_up[0] + resid_up[0]
    factor_up = jnp.dot(delta_up, basis_up, precision=highest, preferred_element_type=jnp.float32)
    new_resid_up = delta_up - jnp.einsum("rk,fk->rf", factor_up, basis_up, precision=highest)
    delta_down = start_down - trained_down[0] + resid_down[0]
    factor_down = jnp.dot(
        delta_down, basis_down, precision=highest, preferred_element_type=jnp.float32
    )
    new_resid_down = delta_down - jnp.einsum(
        "rk,dk->rd", factor_down, basis_down, precision=highest
    )
    norm_delta = start_ln - trained_ln[0]
    summed = lax.psum((factor_sq, factor_up, factor_down, norm_delta), "rep")
    mean_sq = summed[0] / groups
    mean_up = summed[1] / groups
    mean_down = summed[2] / groups
    mean_ln = summed[3] / groups
    new_mom_ln, norm_weights = advance(start_ln, mom_ln, mean_ln)
    outer_sq = jnp.einsum("mrk,mdk->mrd", mean_sq, basis_sq, precision=highest)
    outer_up = jnp.einsum("rk,fk->rf", mean_up, basis_up, precision=highest)
    outer_down = jnp.einsum("rk,dk->rd", mean_down, basis_down, precision=highest)
    new_mom_sq, owned_sq = advance(start_sq, mom_sq, outer_sq)
    new_mom_up, owned_up = advance(start_up, mom_up, outer_up)
    new_mom_down, owned_down = advance(start_down, mom_down, outer_down)
    weights_sq, weights_up, weights_down, weights_ln = (
        lax.all_gather(owned_sq, "shard", axis=1, tiled=True),
        lax.all_gather(owned_up, "shard", axis=0, tiled=True),
        lax.all_gather(owned_down, "shard", axis=0, tiled=True),
        lax.all_gather(norm_weights, "shard", axis=1, tiled=True),
    )
    return (
        new_resid_sq[None],
        new_resid_up[None],
        new_resid_down[None],
        new_mom_sq,
        new_mom_up,
        new_mom_down,
        new_mom_ln,
        weights_sq,
        weights_up,
        weights_down,
        weights_ln,
    )


def solution(mesh):
    placed = (
        P("rep", None, "shard", None),
        P("rep", "shard", None),
        P("rep", "shard", None),
        P("rep", None, "shard"),
        P(None, "shard", None),
        P("shard", None),
        P("shard", None),
        P(None, "shard"),
        P("rep", None, "shard", None),
        P("rep", "shard", None),
        P("rep", "shard", None),
        P(None, "shard", None),
        P("shard", None),
        P("shard", None),
        P(None, "shard"),
        P(),
        P(),
        P(),
    )
    return jax.shard_map(
        on_device,
        mesh=mesh,
        in_specs=placed,
        out_specs=(
            P("rep", None, "shard", None),
            P("rep", "shard", None),
            P("rep", "shard", None),
            P(None, "shard", None),
            P("shard", None),
            P("shard", None),
            P(None, "shard"),
            P(),
            P(),
            P(),
            P(),
        ),
        check_vma=False,
    )
```

profile of v0, /device:TPU:1, one launch (start us, length us, event | category | flops | bytes accessed | tf_op | source)
XLA Modules:
  0.0 201.4 jit_solution(2891028444277751555)
XLA Ops:
  7.2 0.0 copy-start
  7.2 0.0 copy-start.5
  7.2 0.0 copy-start.4
  7.2 0.0 copy-start.6
  7.2 0.0 copy-start.3
  7.2 0.0 copy-start.1
  7.3 0.0 all-gather.5.cloned.1.call-start
  7.3 0.9 bitcast_subtract_fusion.3
  8.2 0.5 copy-done
  8.7 0.0 copy-start.9
  8.7 2.6 %fusion.16 = f32[4,24,64]{2,1,0:T(8,128)} fusion(f32[4,768,64]{1,2,0:T(8,128)S(1)} %copy-done, f32[1,4,24,768]{3,2,1,0:T(8,128)} %param.26, f32[4,24,768]{2,1,0:T(8,128)} %param.22, f32[1,4,24,768]{3,2,1,0:T(8,128)} %param.18), kind=kOutput, calls=%fused_computation.34 | convolution fusion | flops 56770560 | bytes 1695744 | tf_op jit(solution)/shard_map/mrd,mdk->mrk/dot_general | solution.py:39
  11.2 0.0 copy-start.7
  11.2 0.0 copy-start.8
  11.2 2.3 %fusion.18 = f32[96,64]{0,1:T(8,128)} fusion(f32[768,64]{0,1:T(8,128)} %param.35, f32[1,96,768]{2,1,0:T(8,128)} %param.28, f32[96,768]{1,0:T(8,128)} %param.24, f32[1,96,768]{2,1,0:T(8,128)} %param.20), kind=kOutput, calls=%fused_computation.36 | convolution fusion | flops 56770560 | bytes 1105920 | tf_op jit(solution)/shard_map/dot_general | solution.py:45
  13.5 2.1 %fusion.17 = f32[24,64]{1,0:T(8,128)S(1)} fusion(f32[3072,64]{0,1:T(8,128)} %param.34, f32[1,24,3072]{2,1,0:T(8,128)} %param.27, f32[24,3072]{1,0:T(8,128)} %param.23, f32[1,24,3072]{2,1,0:T(8,128)} %param.19), kind=kOutput, calls=%fused_computation.35 | convolution fusion | flops 56770560 | bytes 1677312 | tf_op jit(solution)/shard_map/dot_general | solution.py:42
  15.6 17.3 %all-reduce = (f32[4,24,64]{2,1,0:T(8,128)}, f32[24,64]{1,0:T(8,128)}, f32[96,64]{0,1:T(8,128)}, f32[4,24]{1,0:T(4,128)}) all-reduce(f32[4,24,64]{2,1,0:T(8,128)} %fusion.16, f32[24,64]{1,0:T(8,128)S(1)} %fusion.17, f32[96,64]{0,1:T(8,128)} %fusion.18, f32[4,24]{1,0:T(4,128)S(1)} %bitcast_subtract_fusion.3), channel_id=1, replica_groups=mesh['rep'=4,'shard'=32] {'rep'}, use_global_device_ids=true, to_apply=%region_0.0 | all-reduce | flops 13920 | bytes 111360 | tf_op jit(solution)/shard_map/psum | solution.py:52
  33.0 0.0 copy-start.10
  33.0 0.0 copy-done.5
  33.0 2.3 %subtract_convert_fusion.2 = (bf16[4,24,768]{2,1,0:T(8,128)(2,1)}, f32[4,24,768]{2,1,0:T(8,128)}) fusion(f32[4,24,768]{2,1,0:T(8,128)S(1)} %copy-done.5, f32[4,24,768]{2,1,0:T(8,128)} %param.29, f32[4,768,64]{1,2,0:T(8,128)S(1)} %copy-done, f32[4,24,64]{2,1,0:T(8,128)} %get-tuple-element.11), kind=kOutput, calls=%fused_computation.14 | convolution fusion | flops 57145344 | bytes 1843200 | tf_op jit(solution)/shard_map/mrk,mdk->mrd/dot_general | solution.py:58
  35.3 0.0 all-gather.5.cloned.1.call-update
  35.3 0.0 all-gather.7.cloned.1.call-start
  35.3 0.0 copy-done.3
  35.3 0.0 copy-done.1
  35.4 2.3 %subtract_convert_fusion.1 = (bf16[24,3072]{1,0:T(8,128)(2,1)}, f32[24,3072]{1,0:T(8,128)}) fusion(f32[24,3072]{1,0:T(8,128)S(1)} %copy-done.3, f32[24,3072]{1,0:T(8,128)} %param.30, f32[3072,64]{0,1:T(8,128)S(1)} %copy-done.1, f32[24,64]{1,0:T(8,128)} %get-tuple-element.12), kind=kOutput, calls=%fused_computation.13 | convolution fusion | flops 57140736 | bytes 1824768 | tf_op jit(solution)/shard_map/rk,fk->rf/dot_general | solution.py:59
  37.6 0.0 all-gather.7.cloned.1.call-update
  37.6 0.0 all-gather.9.cloned.1.call-start
  37.7 0.0 copy-done.4
  37.7 0.0 copy-done.6
  37.7 2.2 %subtract_convert_fusion = (bf16[96,768]{1,0:T(8,128)(2,1)}, f32[96,768]{1,0:T(8,128)}) fusion(f32[96,768]{1,0:T(8,128)S(1)} %copy-done.4, f32[96,768]{1,0:T(8,128)} %param.31, f32[768,64]{0,1:T(8,128)S(1)} %copy-done.6, f32[96,64]{0,1:T(8,128)} %get-tuple-element.13), kind=kOutput, calls=%fused_computation.12 | convolution fusion | flops 57145344 | bytes 1253376 | tf_op jit(solution)/shard_map/rk,dk->rd/dot_general | solution.py:60
  39.9 0.0 all-gather.9.cloned.1.call-update
  40.0 0.0 copy-done.10
  40.0 1.3 fusion.12
  41.3 28.7 %all-gather = bf16[32,24,4]{1,2,0:T(4,128)(2,1)S(1)} all-gather(bf16[1,24,4]{1,2,0:T(4,128)(2,1)S(1)} %get-tuple-element.15), channel_id=1, replica_groups=mesh['rep'=4,'shard'=32] {'shard'}, dimensions={0}, use_global_device_ids=true | all-gather | bytes 6336 | tf_op jit(solution)/shard_map/all_gather | solution.py:68
  69.9 0.6 copy.30
  70.6 1.5 reshape.23
  72.0 0.0 copy-done.9
  72.0 2.1 %fusion.1 = f32[1,96,768]{2,1,0:T(8,128)} fusion(f32[96,64]{0,1:T(8,128)} %fusion.18, f32[768,64]{0,1:T(8,128)S(1)} %copy-done.6, f32[1,96,768]{2,1,0:T(8,128)S(1)} %copy-done.9, f32[96,768]{1,0:T(8,128)S(1)} %copy-done.4, f32[1,96,768]{2,1,0:T(8,128)} %param.20), kind=kOutput, calls=%fused_computation.3 | convolution fusion | flops 56844288 | bytes 1400832 | tf_op jit(solution)/shard_map/rk,dk->rd/dot_general | solution.py:48
  74.2 0.0 copy-done.7
  74.2 0.0 copy-done.8
  74.2 1.2 fusion
  75.4 2.3 %fusion.2 = f32[1,4,24,768]{3,2,1,0:T(8,128)} fusion(f32[4,24,64]{2,1,0:T(8,128)} %fusion.16, f32[4,768,64]{1,2,0:T(8,128)S(1)} %copy-done, f32[1,4,24,768]{3,2,1,0:T(8,128)} %param.26, f32[4,24,768]{2,1,0:T(8,128)S(1)} %copy-done.5, f32[1,4,24,768]{3,2,1,0:T(8,128)} %param.18), kind=kOutput, calls=%fused_computation.5 | convolution fusion | flops 56844288 | bytes 1990656 | tf_op jit(solution)/shard_map/mrk,mdk->mrd/dot_general | solution.py:40
  77.7 8.5 %all-gather.5.cloned.1.call-done = bf16[4,768,768]{2,1,0:T(8,128)(2,1)} async-done(((bf16[4,24,768]{2,1,0:T(8,128)(2,1)}), bf16[4,768,768]{2,1,0:T(8,128)(2,1)}) %all-gather.5.cloned.1.call-update) | async-done | bytes 4718608 | tf_op jit(solution)/shard_map/all_gather | solution.py:65
  86.2 49.0 %all-gather.7.cloned.1.call-done = bf16[768,3072]{1,0:T(8,128)(2,1)} async-done(((bf16[24,3072]{1,0:T(8,128)(2,1)}), bf16[768,3072]{1,0:T(8,128)(2,1)}) %all-gather.7.cloned.1.call-update) | async-done | bytes 4718608 | tf_op jit(solution)/shard_map/all_gather | solution.py:66
  135.1 49.0 %all-gather.9.cloned.1.call-done = bf16[3072,768]{1,0:T(8,128)(2,1)} async-done(((bf16[96,768]{1,0:T(8,128)(2,1)}), bf16[3072,768]{1,0:T(8,128)(2,1)}) %all-gather.9.cloned.1.call-update) | async-done | bytes 4718608 | tf_op jit(solution)/shard_map/all_gather | solution.py:67
  184.1 0.0 copy-start.2
  184.1 0.0 slice-start
  184.1 5.2 %copy.34 = bf16[4,768,768]{2,1,0:T(8,128)(2,1)} copy(bf16[4,768,768]{2,1,0:T(8,128)(2,1)} %all-gather.5.cloned.1.call-done) | data formatting | bytes 9437184
  189.3 0.0 copy-done.2
  189.3 0.0 slice-start.1
  189.3 2.4 %copy.35 = bf16[768,3072]{1,0:T(8,128)(2,1)} copy(bf16[768,3072]{1,0:T(8,128)(2,1)S(1)} %copy-done.2) | data formatting | bytes 9437184
  191.7 0.5 slice-done
  192.2 0.5 slice-done.1
  192.7 2.2 %copy.36 = bf16[3072,768]{1,0:T(8,128)(2,1)} copy(bf16[3072,768]{1,0:T(8,128)(2,1)S(1)} %bitcast.64) | data formatting | bytes 9437184
  (1 shorter events, 0.0 us)
Async XLA Ops:
  7.2 1.5 copy-start
  7.2 25.8 %copy-start.5 = (f32[4,24,768]{2,1,0:T(8,128)S(1)}, f32[4,24,768]{2,1,0:T(8,128)}, u32[]{:S(2)}) copy-start(f32[4,24,768]{2,1,0:T(8,128)} %param.22) | copy-start | bytes 884740
  7.2 30.5 %copy-start.4 = (f32[96,768]{1,0:T(8,128)S(1)}, f32[96,768]{1,0:T(8,128)}, u32[]{:S(2)}) copy-start(f32[96,768]{1,0:T(8,128)} %param.24) | copy-start | bytes 884740
  7.2 30.5 %copy-start.6 = (f32[768,64]{0,1:T(8,128)S(1)}, f32[768,64]{0,1:T(8,128)}, u32[]{:S(2)}) copy-start(f32[768,64]{0,1:T(8,128)} %param.35) | copy-start | bytes 589828
  7.2 28.1 %copy-start.3 = (f32[24,3072]{1,0:T(8,128)S(1)}, f32[24,3072]{1,0:T(8,128)}, u32[]{:S(2)}) copy-start(f32[24,3072]{1,0:T(8,128)} %param.23) | copy-start | bytes 884740
  7.2 28.1 %copy-start.1 = (f32[3072,64]{0,1:T(8,128)S(1)}, f32[3072,64]{0,1:T(8,128)}, u32[]{:S(2)}) copy-start(f32[3072,64]{0,1:T(8,128)} %param.34) | copy-start | bytes 2359300
  7.3 78.9 %all-gather.5.cloned.1.call-start = ((), (), s32[]{:S(2)}) async-start(), calls=%async_computation | async-start | bytes 4866048 | tf_op jit(solution)/shard_map/all_gather | solution.py:65
  8.7 63.3 %copy-start.9 = (f32[1,96,768]{2,1,0:T(8,128)S(1)}, f32[1,96,768]{2,1,0:T(8,128)}, u32[]{:S(2)}) copy-start(f32[1,96,768]{2,1,0:T(8,128)} %param.28) | copy-start | bytes 884740
  11.2 62.9 %copy-start.7 = (f32[1,24,3072]{2,1,0:T(8,128)S(1)}, f32[1,24,3072]{2,1,0:T(8,128)}, u32[]{:S(2)}) copy-start(f32[1,24,3072]{2,1,0:T(8,128)} %param.27) | copy-start | bytes 884740
  11.2 62.9 %copy-start.8 = (f32[1,24,3072]{2,1,0:T(8,128)S(1)}, f32[1,24,3072]{2,1,0:T(8,128)}, u32[]{:S(2)}) copy-start(f32[1,24,3072]{2,1,0:T(8,128)} %param.19) | copy-start | bytes 884740
  33.0 7.0 %copy-start.10 = (f32[4,24]{1,0:T(4,128)S(1)}, f32[4,24]{1,0:T(4,128)}, u32[]{:S(2)}) copy-start(f32[4,24]{1,0:T(4,128)} %get-tuple-element.14) | copy-start | bytes 1156
  35.3 99.8 %all-gather.7.cloned.1.call-start = ((), (), s32[]{:S(2)}) async-start(), calls=%async_computation.1 | async-start | bytes 4866048 | tf_op jit(solution)/shard_map/all_gather | solution.py:66
  37.6 146.5 %all-gather.9.cloned.1.call-start = ((), (), s32[]{:S(2)}) async-start(), calls=%async_computation.2 | async-start | bytes 4866048 | tf_op jit(solution)/shard_map/all_gather | solution.py:67
  184.1 5.2 %copy-start.2 = (bf16[768,3072]{1,0:T(8,128)(2,1)S(1)}, bf16[768,3072]{1,0:T(8,128)(2,1)}, u32[]{:S(2)}) copy-start(bf16[768,3072]{1,0:T(8,128)(2,1)} %all-gather.7.cloned.1.call-done) | copy-start | bytes 14155780
  184.1 8.0 %slice-start = ((s8[4718592]{0:T(1024)(128)(4,1)}), s8[4194304]{0:T(1024)(128)(4,1)S(1)}, s32[]{:S(2)}) async-start(s8[4718592]{0:T(1024)(128)(4,1)} %bitcast.63), calls=%async_computation.3 | async-start | bytes 8388608
  189.3 3.4 %slice-start.1 = ((s8[4718592]{0:T(1024)(128)(4,1)}), s8[524288]{0:T(1024)(128)(4,1)S(1)}, s32[]{:S(2)}) async-start(s8[4718592]{0:T(1024)(128)(4,1)} %bitcast.63), calls=%async_computation.4 | async-start | bytes 1048576
Sparse Core Ops, SparseCore 0:
  35.4 50.7 all-gather.4
  89.0 46.0 all-gather.6
  137.9 46.1 all-gather.8
where the time goes:
time: 202 us; the launch traced here: 201 us
  waiting for transfers between devices  106 us (52%)
  blocking collectives  46 us (23%)
  matrix products  19.4 us (10%)
  between operations  13.9 us (7%)
  local copies, waits for them, and re-layouts  13.4 us (7%)
  other arithmetic  2.13 us (1%)
    all_gather x1, waiting for transfers between devices, on_device(): lax.all_gather(owned_down, 'shard', axis=0, tiled=True)  49 us
    all_gather x1, waiting for transfers between devices, on_device(): lax.all_gather(owned_up, 'shard', axis=0, tiled=True)  49 us
    all_gather x1, blocking collectives, on_device(): lax.all_gather(norm_weights, 'shard', axis=1, tiled=True)  28.7 us
    psum x1, blocking collectives, on_device(): summed = lax.psum((factor_sq, factor_up, factor_down, norm_delta), 'rep')  17.3 us
    unnamed x30, local copies, waits for them, and re-layouts  12.8 us
    all_gather x1, waiting for transfers between devices, on_device(): lax.all_gather(owned_sq, 'shard', axis=1, tiled=True)  8.47 us
  transfers between devices with their start and end apart: 3, of which 3 were waited for; matrix products, arithmetic and copies ran while one was open for 7% of the time, Pallas kernels for 0%

commit v1 on v0

--- a/solution.py
+++ b/solution.py
@@ -5,6 +5,14 @@
 
 moment_coef = 0.9
 outer_rate = 0.7
+
+
+def gather_by_exchange(value, axis, dim):
+    peers = lax.axis_size(axis)
+    repeats = [peers if d == dim else 1 for d in range(value.ndim)]
+    return lax.all_to_all(
+        jnp.tile(value, repeats), axis, split_axis=dim, concat_axis=dim, tiled=True
+    )
 
 
 def advance(start, moment, outer):
@@ -63,7 +71,7 @@
     new_mom_down, owned_down = advance(start_down, mom_down, outer_down)
     weights_sq, weights_up, weights_down, weights_ln = (
         lax.all_gather(owned_sq, "shard", axis=1, tiled=True),
-        lax.all_gather(owned_up, "shard", axis=0, tiled=True),
+        gather_by_exchange(owned_up, "shard", 0),
         lax.all_gather(owned_down, "shard", axis=0, tiled=True),
         lax.all_gather(norm_weights, "shard", axis=1, tiled=True),
     )

time: 202 us -> 189 us (0.936)
  waiting for transfers between devices: 106 us -> 28.1 us
  blocking collectives: 46 us -> 99.4 us
  starting transfers between devices: 0.12 us -> 11.8 us
  local copies, waits for them, and re-layouts: 13.4 us -> 17.3 us
  matrix products: 19.4 us -> 16 us
    all_gather x1, blocking collectives: 28.7 us -> 82.6 us  [on_device(): lax.all_gather(norm_weights, 'shard', axis=1, tiled=True)]
    all_gather x1 -> x0, waiting for transfers between devices: 49 us -> none  [on_device(): lax.all_gather(owned_up, 'shard', axis=0, tiled=True)]
    all_gather x1, waiting for transfers between devices: 49 us -> 28.1 us  [on_device(): lax.all_gather(owned_down, 'shard', axis=0, tiled=True)]
    all_to_all x0 -> x1, starting transfers between devices: none -> 11.7 us  [gather_by_exchange(): lax.all_to_all(jnp.tile(value, repeats), axis, split_axis=dim, concat_axi...]
    all_gather x1, waiting for transfers between devices: 8.47 us -> 0.01 us  [on_device(): lax.all_gather(owned_sq, 'shard', axis=1, tiled=True)]
    another operation x0 -> x1, local copies, waits for them, and re-layouts: none -> 2.77 us  [gather_by_exchange(): jnp.tile(value, repeats)]
    unnamed x30 -> x36, local copies, waits for them, and re-layouts: 12.8 us -> 13.9 us
  transfers between devices with their start and end apart: 3 -> 3, of which waited for: 3 -> 1; matrix products, arithmetic and copies ran while one was open for 7% -> 8% of each run, Pallas kernels for 0% -> 0%
where the time goes in v1:
time: 189 us
  blocking collectives  99.4 us (53%)
  waiting for transfers between devices  28.1 us (15%)
  local copies, waits for them, and re-layouts  17.3 us (9%)
  matrix products  16 us (8%)
  between operations  14.2 us (8%)
  starting transfers between devices  11.8 us (6%)
  other arithmetic  2.13 us (1%)
    all_gather x1, blocking collectives, on_device(): lax.all_gather(norm_weights, 'shard', axis=1, tiled=True)  82.6 us
    all_gather x1, waiting for transfers between devices, on_device(): lax.all_gather(owned_down, 'shard', axis=0, tiled=True)  28.1 us
    psum x1, blocking collectives, on_device(): summed = lax.psum((factor_sq, factor_up, factor_down, norm_delta), 'rep')  16.8 us
    unnamed x36, local copies, waits for them, and re-layouts  13.9 us
    all_to_all x1, starting transfers between devices, gather_by_exchange(): lax.all_to_all(jnp.tile(value, repeats), axis, split_axis=dim, concat_axi...  11.7 us
  transfers between devices with their start and end apart: 3, of which 1 were waited for; matrix products, arithmetic and copies ran while one was open for 8% of the time, Pallas kernels for 0%

profile of v1, /device:TPU:1, one launch (start us, length us, event | category | flops | bytes accessed | tf_op | source)
XLA Modules:
  0.0 189.0 jit_solution(14513160146924526255)
XLA Ops:
  7.2 0.0 copy-start
  7.2 0.0 copy-start.4
  7.2 0.0 copy-start.3
  7.2 0.0 copy-start.5
  7.2 0.0 copy-start.2
  7.2 0.0 copy-start.1
  7.3 0.0 copy-start.10
  7.3 0.0 copy-start.11
  7.3 0.0 all-gather.4.cloned.1.call-start
  7.3 0.8 bitcast_subtract_fusion.3
  8.2 0.3 copy-done
  8.5 1.9 %fusion.16 = f32[4,24,64]{2,1,0:T(8,128)S(1)} fusion(f32[4,768,64]{1,2,0:T(8,128)S(1)} %copy-done, f32[1,4,24,768]{3,2,1,0:T(8,128)} %param.26, f32[4,24,768]{2,1,0:T(8,128)} %param.22, f32[1,4,24,768]{3,2,1,0:T(8,128)} %param.18), kind=kOutput, calls=%fused_computation.34 | convolution fusion | flops 56770560 | bytes 1695744 | tf_op jit(solution)/shard_map/mrd,mdk->mrk/dot_general | solution.py:47
  10.4 0.0 copy-start.9
  10.4 1.6 fusion.18
  12.0 0.0 copy-start.12
  12.0 2.1 %fusion.17 = f32[24,64]{1,0:T(8,128)S(1)} fusion(f32[3072,64]{0,1:T(8,128)} %param.34, f32[1,24,3072]{2,1,0:T(8,128)} %param.27, f32[24,3072]{1,0:T(8,128)} %param.23, f32[1,24,3072]{2,1,0:T(8,128)} %param.19), kind=kOutput, calls=%fused_computation.35 | convolution fusion | flops 56770560 | bytes 1677312 | tf_op jit(solution)/shard_map/dot_general | solution.py:50
  14.2 16.8 %all-reduce = (f32[4,24,64]{2,1,0:T(8,128)S(1)}, f32[24,64]{1,0:T(8,128)S(1)}, f32[96,64]{0,1:T(8,128)S(1)}, f32[4,24]{1,0:T(4,128)}) all-reduce(f32[4,24,64]{2,1,0:T(8,128)S(1)} %fusion.16, f32[24,64]{1,0:T(8,128)S(1)} %fusion.17, f32[96,64]{0,1:T(8,128)S(1)} %fusion.18, ...), channel_id=1, replica_groups=mesh['rep'=4,'shard'=32] {'rep'}, use_global_device_ids=true, to_apply=%region_0.0 | all-reduce | flops 13920 | bytes 111360 | tf_op jit(solution)/shard_map/psum | solution.py:60
  31.0 0.0 copy-done.4
  31.0 0.0 copy-done.10
  31.0 1.3 subtract_convert_fusion.2
  32.3 0.0 all-gather.4.cloned.1.call-update
  32.3 0.0 all-gather.6.cloned.1.call-start
  32.4 0.0 copy-done.3
  32.4 0.0 copy-done.5
  32.4 0.0 copy-done.11
  32.4 1.2 subtract_convert_fusion
  33.6 0.0 all-gather.6.cloned.1.call-update
  33.7 0.0 copy-done.2
  33.7 0.0 copy-done.1
  33.7 2.2 %subtract_convert_fusion.1 = (bf16[24,3072]{1,0:T(8,128)(2,1)S(1)}, f32[24,3072]{1,0:T(8,128)}) fusion(f32[24,3072]{1,0:T(8,128)S(1)} %copy-done.2, f32[24,3072]{1,0:T(8,128)} %param.30, f32[3072,64]{0,1:T(8,128)S(1)} %copy-done.1, f32[24,64]{1,0:T(8,128)S(1)} %get-tuple-element.12), kind=kOutput, calls=%fused_computation.13 | convolution fusion | flops 57140736 | bytes 1824768 | tf_op jit(solution)/shard_map/rk,fk->rf/dot_general | solution.py:67
  35.9 0.0 copy-done.9
  35.9 0.0 copy-done.12
  35.9 2.8 %tile.2 = bf16[32,24,3072]{2,1,0:T(8,128)(2,1)} broadcast(bf16[24,3072]{1,0:T(8,128)(2,1)S(1)} %get-tuple-element.19), dimensions={1,2} | broadcast | bytes 4866048 | tf_op jit(solution)/shard_map/tile | solution.py:14
  38.7 0.0 copy-start.13
  38.7 0.0 copy-start.8
  38.7 0.0 copy-start.6
  38.7 0.0 copy-start.7
  38.7 11.7 %all-to-all-start = ((bf16[32,24,3072]{2,1,0:T(8,128)(2,1)}), bf16[32,24,3072]{2,1,0:T(8,128)(2,1)}, u32[]{:S(2)}, u32[]{:S(2)}) async-start(bf16[32,24,3072]{2,1,0:T(8,128)(2,1)} %tile.2), calls=%async_computation | async-start | bytes 9437184 | tf_op jit(solution)/shard_map/all_to_all | solution.py:13
  50.4 0.0 copy-done.13
  50.4 1.3 fusion.12
  51.7 82.6 %all-gather = bf16[32,24,4]{1,2,0:T(4,128)(2,1)S(1)} all-gather(bf16[1,24,4]{1,2,0:T(4,128)(2,1)S(1)} %get-tuple-element.15), channel_id=1, replica_groups=mesh['rep'=4,'shard'=32] {'shard'}, dimensions={0}, use_global_device_ids=true | all-gather | bytes 6336 | tf_op jit(solution)/shard_map/all_gather | solution.py:76
  134.2 0.6 copy.30
  134.9 1.5 reshape.30
  136.3 0.0 copy-done.8
  136.3 2.1 %fusion.1 = f32[1,96,768]{2,1,0:T(8,128)} fusion(f32[96,64]{0,1:T(8,128)} %copy-done.12, f32[768,64]{0,1:T(8,128)S(1)} %copy-done.5, f32[1,96,768]{2,1,0:T(8,128)S(1)} %copy-done.8, f32[96,768]{1,0:T(8,128)S(1)} %copy-done.3, f32[1,96,768]{2,1,0:T(8,128)} %param.20), kind=kOutput, calls=%fused_computation.3 | convolution fusion | flops 56844288 | bytes 1400832 | tf_op jit(solution)/shard_map/rk,dk->rd/dot_general | solution.py:56
  138.5 0.0 copy-done.6
  138.5 0.0 copy-done.7
  138.5 1.2 fusion
  139.7 2.3 %fusion.2 = f32[1,4,24,768]{3,2,1,0:T(8,128)} fusion(f32[4,24,64]{2,1,0:T(8,128)} %copy-done.9, f32[4,768,64]{1,2,0:T(8,128)S(1)} %copy-done, f32[1,4,24,768]{3,2,1,0:T(8,128)} %param.26, f32[4,24,768]{2,1,0:T(8,128)S(1)} %copy-done.4, f32[1,4,24,768]{3,2,1,0:T(8,128)} %param.18), kind=kOutput, calls=%fused_computation.5 | convolution fusion | flops 56844288 | bytes 1990656 | tf_op jit(solution)/shard_map/mrk,mdk->mrd/dot_general | solution.py:48
  142.0 0.0 all-to-all-done
  142.0 0.0 all-gather.4.cloned.1.call-done
  142.0 28.1 %all-gather.6.cloned.1.call-done = bf16[3072,768]{1,0:T(8,128)(2,1)} async-done(((bf16[96,768]{1,0:T(8,128)(2,1)}), bf16[3072,768]{1,0:T(8,128)(2,1)}) %all-gather.6.cloned.1.call-update) | async-done | bytes 4718608 | tf_op jit(solution)/shard_map/all_gather | solution.py:75
  170.1 0.0 slice-start
  170.1 5.0 %copy.34 = bf16[4,768,768]{2,1,0:T(8,128)(2,1)} copy(bf16[4,768,768]{2,1,0:T(8,128)(2,1)} %all-gather.4.cloned.1.call-done) | data formatting | bytes 9437184
  175.0 0.0 slice-start.1
  175.0 4.9 %copy.35 = bf16[768,3072]{1,0:T(8,128)(2,1)} copy(bf16[768,3072]{1,0:T(8,128)(2,1)} %bitcast.10) | data formatting | bytes 9437184
  179.9 0.0 slice-done
  179.9 0.0 slice-done.1
  179.9 2.2 %copy.36 = bf16[3072,768]{1,0:T(8,128)(2,1)} copy(bf16[3072,768]{1,0:T(8,128)(2,1)S(1)} %bitcast.65) | data formatting | bytes 9437184
  (1 shorter events, 0.0 us)
Async XLA Ops:
  7.2 1.3 copy-start
  7.2 23.8 %copy-start.4 = (f32[4,24,768]{2,1,0:T(8,128)S(1)}, f32[4,24,768]{2,1,0:T(8,128)}, u32[]{:S(2)}) copy-start(f32[4,24,768]{2,1,0:T(8,128)} %param.22) | copy-start | bytes 884740
  7.2 25.2 %copy-start.3 = (f32[96,768]{1,0:T(8,128)S(1)}, f32[96,768]{1,0:T(8,128)}, u32[]{:S(2)}) copy-start(f32[96,768]{1,0:T(8,128)} %param.24) | copy-start | bytes 884740
  7.2 25.2 %copy-start.5 = (f32[768,64]{0,1:T(8,128)S(1)}, f32[768,64]{0,1:T(8,128)}, u32[]{:S(2)}) copy-start(f32[768,64]{0,1:T(8,128)} %param.35) | copy-start | bytes 589828
  7.2 26.4 %copy-start.2 = (f32[24,3072]{1,0:T(8,128)S(1)}, f32[24,3072]{1,0:T(8,128)}, u32[]{:S(2)}) copy-start(f32[24,3072]{1,0:T(8,128)} %param.23) | copy-start | bytes 884740
  7.2 26.4 %copy-start.1 = (f32[3072,64]{0,1:T(8,128)S(1)}, f32[3072,64]{0,1:T(8,128)}, u32[]{:S(2)}) copy-start(f32[3072,64]{0,1:T(8,128)} %param.34) | copy-start | bytes 2359300
  7.3 23.7 %copy-start.10 = (f32[4,24,768]{2,1,0:T(8,128)S(1)}, f32[4,24,768]{2,1,0:T(8,128)}, u32[]{:S(2)}) copy-start(f32[4,24,768]{2,1,0:T(8,128)} %param.29) | copy-start | bytes 884740
  7.3 25.1 %copy-start.11 = (f32[96,768]{1,0:T(8,128)S(1)}, f32[96,768]{1,0:T(8,128)}, u32[]{:S(2)}) copy-start(f32[96,768]{1,0:T(8,128)} %param.31) | copy-start | bytes 884740
  7.3 134.7 %all-gather.4.cloned.1.call-start = ((), (), s32[]{:S(2)}) async-start(), calls=%async_computation.1 | async-start | bytes 4866048 | tf_op jit(solution)/shard_map/all_gather | solution.py:73
  10.4 25.5 %copy-start.9 = (f32[4,24,64]{2,1,0:T(8,128)}, f32[4,24,64]{2,1,0:T(8,128)S(1)}, u32[]{:S(2)}) copy-start(f32[4,24,64]{2,1,0:T(8,128)S(1)} %fusion.16) | copy-start | bytes 73732
  12.0 23.9 %copy-start.12 = (f32[96,64]{0,1:T(8,128)}, f32[96,64]{0,1:T(8,128)S(1)}, u32[]{:S(2)}) copy-start(f32[96,64]{0,1:T(8,128)S(1)} %fusion.18) | copy-start | bytes 73732
  32.3 137.7 %all-gather.6.cloned.1.call-start = ((), (), s32[]{:S(2)}) async-start(), calls=%async_computation.2 | async-start | bytes 4866048 | tf_op jit(solution)/shard_map/all_gather | solution.py:75
  38.7 11.7 %copy-start.13 = (f32[4,24]{1,0:T(4,128)S(1)}, f32[4,24]{1,0:T(4,128)}, u32[]{:S(2)}) copy-start(f32[4,24]{1,0:T(4,128)} %param.25) | copy-start | bytes 1156
  38.7 97.7 %copy-start.8 = (f32[1,96,768]{2,1,0:T(8,128)S(1)}, f32[1,96,768]{2,1,0:T(8,128)}, u32[]{:S(2)}) copy-start(f32[1,96,768]{2,1,0:T(8,128)} %param.28) | copy-start | bytes 884740
  38.7 99.8 %copy-start.6 = (f32[1,24,3072]{2,1,0:T(8,128)S(1)}, f32[1,24,3072]{2,1,0:T(8,128)}, u32[]{:S(2)}) copy-start(f32[1,24,3072]{2,1,0:T(8,128)} %param.27) | copy-start | bytes 884740
  38.7 99.8 %copy-start.7 = (f32[1,24,3072]{2,1,0:T(8,128)S(1)}, f32[1,24,3072]{2,1,0:T(8,128)}, u32[]{:S(2)}) copy-start(f32[1,24,3072]{2,1,0:T(8,128)} %param.19) | copy-start | bytes 884740
  38.7 103.3 %all-to-all-start = ((bf16[32,24,3072]{2,1,0:T(8,128)(2,1)}), bf16[32,24,3072]{2,1,0:T(8,128)(2,1)}, u32[]{:S(2)}, u32[]{:S(2)}) async-start(bf16[32,24,3072]{2,1,0:T(8,128)(2,1)} %tile.2), calls=%async_computation | async-start | bytes 9437184 | tf_op jit(solution)/shard_map/all_to_all | solution.py:13
  170.1 9.9 %slice-start = ((s8[4718592]{0:T(1024)(128)(4,1)}), s8[4194304]{0:T(1024)(128)(4,1)S(1)}, s32[]{:S(2)}) async-start(s8[4718592]{0:T(1024)(128)(4,1)} %bitcast.64), calls=%async_computation.3 | async-start | bytes 8388608
  175.0 4.9 %slice-start.1 = ((s8[4718592]{0:T(1024)(128)(4,1)}), s8[524288]{0:T(1024)(128)(4,1)S(1)}, s32[]{:S(2)}) async-start(s8[4718592]{0:T(1024)(128)(4,1)} %bitcast.64), calls=%async_computation.4 | async-start | bytes 1048576
Sparse Core Ops, SparseCore 0:
  32.4 88.8 all-gather.3
  124.1 45.8 all-gather.5
